TPU v7x, 256 devices: a whole 4x4x8 slice. The times are simulated.
256 devices in a mesh: layer: 64 (over y, z, core), blk: 4 (over x).
Axes of the slice: x: 4, y: 4, z: 8, core: 2. Of those that a mesh axis runs over, the one named last changes fastest.
Arguments:
- mode_matrix: bfloat16 [128, 512, 512], P(None, 'layer', 'blk'), may hold values from -1 to 1, as said below
- decay_rate: bfloat16 [128, 512], P(None, 'layer'), may hold values from 0.0009994507 to 0.29882812
- facet_refl: bfloat16 [128, 512], P(None, 'layer'), may hold values from -0.796875 to 0.796875
Outputs:
- prefix: bfloat16 [64, 4, 512, 512], P('layer', None, 'blk')
Inputs may be any that keep to these rules, and one draw needn't show every extreme that they name: `mode_matrix`: each layer's matrix has orthonormal columns up to the rounding to bfloat16.
All inputs are finite; a program needn't handle non-finite values.
Results may differ from a plain program's by a relative error of at most 0.0045.
The roundings to bfloat16 on the way count: a program that leaves them out, or rounds other values in their place, can miss the bound.
Values may be sent and summed in bfloat16 or wider, within the bound.
No kernel may reach another device: no remote copies, remote signals or barrier semaphores. Data moves between devices by JAX's collectives and lax.ppermute only.
A program may use at most 64 MiB of HBM per device.

v0:
```python
import jax
import jax.numpy as jnp
from jax import lax
from jax.sharding import PartitionSpec as P

HARM = 512
REFL = 4


def passed_along(value, axis, steps):
    count = lax.axis_size(axis)
    first, last = (max(0, -steps), min(count, count - steps))
    return lax.ppermute(value, axis, [(source, source + steps) for source in range(first, last)])


def times_f32(left_op, right_op):
    return jnp.dot(left_op, right_op, preferred_element_type=jnp.float32)


def star_rows(upper_near, upper_far, lower_near, lower_rows):
    coupling_down = times_f32(lower_near[0], upper_far[1]).astype(jnp.bfloat16)
    coupling_up = times_f32(upper_far[1], lower_near[0]).astype(jnp.bfloat16)
    left_sum = upper_near[1]
    for repeat in range(REFL):
        left_sum = (upper_near[1] + times_f32(left_sum, coupling_down)).astype(jnp.bfloat16)
    right_sum = lower_rows[0]
    for repeat in range(REFL):
        right_sum = (lower_rows[0] + times_f32(right_sum, coupling_up)).astype(jnp.bfloat16)
    left_mid = times_f32(left_sum, lower_near[0]).astype(jnp.bfloat16)
    right_mid = times_f32(right_sum, upper_far[1]).astype(jnp.bfloat16)
    new_refl = (upper_near[0] + times_f32(left_mid, upper_far[0])).astype(jnp.bfloat16)
    new_back = times_f32(left_sum, lower_near[1]).astype(jnp.bfloat16)
    new_fore = times_f32(right_sum, upper_far[0]).astype(jnp.bfloat16)
    new_under = (lower_rows[1] + times_f32(right_mid, lower_near[1])).astype(jnp.bfloat16)
    return jnp.stack([new_refl, new_back, new_fore, new_under])


def on_device(mode_matrix, decay_rate, facet_refl):
    relayed_modes, relayed_decay, relayed_refl = (
        lax.all_to_all(mode_matrix, "layer", split_axis=0, concat_axis=1, tiled=True),
        lax.all_to_all(decay_rate, "layer", split_axis=0, concat_axis=1, tiled=True),
        lax.all_to_all(facet_refl, "layer", split_axis=0, concat_axis=1, tiled=True),
    )
    block_index = lax.axis_index("blk")
    row_count = HARM // lax.axis_size("blk")
    row_start = block_index * row_count
    refl_full = relayed_refl.astype(jnp.float32)
    transmit = jnp.sqrt(1.0 - refl_full * refl_full) * jnp.exp(-relayed_decay.astype(jnp.float32))
    mode_piece = lax.all_gather(relayed_modes, "blk", axis=2, tiled=True)
    piece_wide = mode_piece.astype(jnp.float32)
    scaled_refl = (piece_wide * refl_full[:, None, :]).astype(jnp.bfloat16)
    scaled_tran = (piece_wide * transmit[:, None, :]).astype(jnp.bfloat16)
    own_rows = lax.dynamic_slice_in_dim(mode_piece, row_start, row_count, 1)
    refl_part = jnp.einsum(
        "lhm,lkm->lhk", own_rows, scaled_refl, preferred_element_type=jnp.float32
    )
    tran_part = jnp.einsum(
        "lhm,lkm->lhk", own_rows, scaled_tran, preferred_element_type=jnp.float32
    )
    refl_rows = refl_part.astype(jnp.bfloat16)
    tran_rows = tran_part.astype(jnp.bfloat16)
    layer_rows = jnp.stack([refl_rows, tran_rows, tran_rows, -refl_rows], axis=1)
    layer_pair = lax.all_gather(
        jnp.stack([refl_rows, tran_rows], axis=1), "blk", axis=2, tiled=True
    )
    rows_now = layer_rows[0]
    full_now = jnp.stack([layer_pair[0, 0], layer_pair[0, 1], layer_pair[0, 1], -layer_pair[0, 0]])
    rows_now = star_rows(rows_now[0:2], full_now[2:4], layer_pair[1], layer_rows[1, 2:4])
    full_now = lax.all_gather(rows_now, "blk", axis=1, tiled=True)
    group_index = lax.axis_index("layer")
    level_count = lax.axis_size("layer").bit_length() - 1
    for section_level in range(level_count):
        distance = 1 << section_level
        upper_whole = passed_along(full_now, "layer", distance)
        upper_near = lax.dynamic_slice_in_dim(upper_whole[0:2], row_start, row_count, 1)
        upper_far = upper_whole[2:4]
        combined = star_rows(upper_near, upper_far, full_now[0:2], rows_now[2:4])
        rows_now = jnp.where(group_index >= distance, combined, rows_now)
        if section_level + 1 < level_count:
            full_now = lax.all_gather(rows_now, "blk", axis=1, tiled=True)
    return rows_now[None]


def solution(mesh):
    placed = (P(None, "layer", "blk"), P(None, "layer"), P(None, "layer"))
    return jax.shard_map(
        on_device,
        mesh=mesh,
        in_specs=placed,
        out_specs=P("layer", None, "blk", None),
        check_vma=False,
    )
```

profile of v0, /device:TPU:16, one launch (start us, length us, event | category | flops | bytes accessed | tf_op | source)
XLA Modules:
  0.0 783.8 jit_solution(11975169473791905162)
XLA Ops:
  6.5 23.6 %all_to_all.44 = bf16[128,8,128]{2,1,0:T(8,128)(2,1)S(1)} all-to-all(bf16[128,8,128]{2,1,0:T(8,128)(2,1)} %param.3), channel_id=1, replica_groups=mesh['layer'=64,'blk'=4] {'layer'}, dimensions={0} | all-to-all | bytes 524288 | tf_op jit(solution)/shard_map/all_to_all | solution.py:40
  32.3 6.5 all-to-all-start.1
  40.2 6.3 all-to-all-done.1
  46.5 6.4 all-to-all-start.2
  53.1 7.5 all-to-all-done.2
  65.5 30.2 %all-gather.11.cloned.1.call-done = bf16[2,2,512,512]{3,2,0,1:T(8,128)(2,1)} async-done(((bf16[2,2,128,512]{3,2,0,1:T(8,128)(2,1)}), bf16[2,2,512,512]{3,2,0,1:T(8,128)(2,1)}) %all-gather.11.cloned.1.call-update) | async-done | bytes 2097168 | tf_op jit(solution)/shard_map/all_gather | solution.py:63
  101.8 33.5 %all-gather.13.cloned.1.call-done = bf16[4,512,512]{2,1,0:T(8,128)(2,1)} async-done(((bf16[4,128,512]{2,1,0:T(8,128)(2,1)}), bf16[4,512,512]{2,1,0:T(8,128)(2,1)}) %all-gather.13.cloned.1.call-update) | async-done | bytes 2097168 | tf_op jit(solution)/shard_map/all_gather | solution.py:69
  137.3 27.7 %collective-permute-done = bf16[4,512,512]{2,1,0:T(8,128)(2,1)S(1)} collective-permute-done((bf16[4,512,512]{2,1,0:T(8,128)(2,1)}, bf16[4,512,512]{2,1,0:T(8,128)(2,1)S(1)}, u32[]{:S(2)}, u32[]{:S(2)}) %collective-permute-start) | collective-permute-done | bytes 2097184 | tf_op jit(solution)/shard_map/ppermute | solution.py:13
  178.0 32.6 %all-gather.15.cloned.1.call-done = bf16[4,512,512]{2,1,0:T(8,128)(2,1)} async-done(((bf16[4,128,512]{2,1,0:T(8,128)(2,1)}), bf16[4,512,512]{2,1,0:T(8,128)(2,1)}) %all-gather.15.cloned.1.call-update) | async-done | bytes 2097168 | tf_op jit(solution)/shard_map/all_gather | solution.py:80
  210.7 3.5 collective-permute-start.1
  214.1 48.2 %collective-permute-done.1 = bf16[4,512,512]{2,1,0:T(8,128)(2,1)} collective-permute-done((bf16[4,512,512]{2,1,0:T(8,128)(2,1)}, bf16[4,512,512]{2,1,0:T(8,128)(2,1)}, u32[]{:S(2)}, u32[]{:S(2)}) %collective-permute-start.1) | collective-permute-done | bytes 2097184 | tf_op jit(solution)/shard_map/ppermute | solution.py:13
  275.4 32.6 %all-gather.17.cloned.1.call-done = bf16[4,512,512]{2,1,0:T(8,128)(2,1)} async-done(((bf16[4,128,512]{2,1,0:T(8,128)(2,1)}), bf16[4,512,512]{2,1,0:T(8,128)(2,1)}) %all-gather.17.cloned.1.call-update) | async-done | bytes 2097168 | tf_op jit(solution)/shard_map/all_gather | solution.py:80
  308.1 4.6 collective-permute-start.2
  312.7 93.8 %collective-permute-done.2 = bf16[4,512,512]{2,1,0:T(8,128)(2,1)} collective-permute-done((bf16[4,512,512]{2,1,0:T(8,128)(2,1)}, bf16[4,512,512]{2,1,0:T(8,128)(2,1)}, u32[]{:S(2)}, u32[]{:S(2)}) %collective-permute-start.2) | collective-permute-done | bytes 2097184 | tf_op jit(solution)/shard_map/ppermute | solution.py:13
  421.0 32.6 %all-gather.19.cloned.1.call-done = bf16[4,512,512]{2,1,0:T(8,128)(2,1)} async-done(((bf16[4,128,512]{2,1,0:T(8,128)(2,1)}), bf16[4,512,512]{2,1,0:T(8,128)(2,1)}) %all-gather.19.cloned.1.call-update) | async-done | bytes 2097168 | tf_op jit(solution)/shard_map/all_gather | solution.py:80
  453.6 7.6 collective-permute-start.3
  461.3 80.8 %collective-permute-done.3 = bf16[4,512,512]{2,1,0:T(8,128)(2,1)} collective-permute-done((bf16[4,512,512]{2,1,0:T(8,128)(2,1)}, bf16[4,512,512]{2,1,0:T(8,128)(2,1)}, u32[]{:S(2)}, u32[]{:S(2)}) %collective-permute-start.3) | collective-permute-done | bytes 2097184 | tf_op jit(solution)/shard_map/ppermute | solution.py:13
  559.2 44.1 %all-gather.21.cloned.1.call-done = bf16[4,512,512]{2,1,0:T(8,128)(2,1)} async-done(((bf16[4,128,512]{2,1,0:T(8,128)(2,1)}), bf16[4,512,512]{2,1,0:T(8,128)(2,1)}) %all-gather.21.cloned.1.call-update) | async-done | bytes 2097168 | tf_op jit(solution)/shard_map/all_gather | solution.py:80
  603.4 3.1 collective-permute-start.4
  606.5 46.5 %collective-permute-done.4 = bf16[4,512,512]{2,1,0:T(8,128)(2,1)} collective-permute-done((bf16[4,512,512]{2,1,0:T(8,128)(2,1)}, bf16[4,512,512]{2,1,0:T(8,128)(2,1)}, u32[]{:S(2)}, u32[]{:S(2)}) %collective-permute-start.4) | collective-permute-done | bytes 2097184 | tf_op jit(solution)/shard_map/ppermute | solution.py:13
  662.0 2.4 fusion.32
  672.9 33.6 %all-gather.23.cloned.1.call-done = bf16[4,512,512]{2,1,0:T(8,128)(2,1)} async-done(((bf16[4,128,512]{2,1,0:T(8,128)(2,1)}), bf16[4,512,512]{2,1,0:T(8,128)(2,1)}) %all-gather.23.cloned.1.call-update) | async-done | bytes 2097168 | tf_op jit(solution)/shard_map/all_gather | solution.py:80
  707.7 49.8 %collective-permute-done.5 = bf16[4,512,512]{2,1,0:T(8,128)(2,1)} collective-permute-done((bf16[4,512,512]{2,1,0:T(8,128)(2,1)}, bf16[4,512,512]{2,1,0:T(8,128)(2,1)}, u32[]{:S(2)}, u32[]{:S(2)}) %collective-permute-start.5) | collective-permute-done | bytes 2097184 | tf_op jit(solution)/shard_map/ppermute | solution.py:13
  766.6 2.4 fusion.68
  (160 shorter events, 109.6 us)
Async XLA Ops:
  6.5 54.4 %all-gather.9.cloned.1.call-start = ((), (), s32[]{:S(2)}) async-start(), calls=%async_computation.3 | async-start | bytes 1310720 | tf_op jit(solution)/shard_map/all_gather | solution.py:49
  32.3 14.2 %all-to-all-start.1 = ((bf16[64,2,8]{2,1,0:T(2,128)(2,1)}), bf16[64,2,8]{2,1,0:T(2,128)(2,1)S(1)}, u32[]{:S(2)}, u32[]{:S(2)}) async-start(bf16[64,2,8]{2,1,0:T(2,128)(2,1)} %bitcast.3), calls=%async_computation.1 | async-start | bytes 65536 | tf_op jit(solution)/shard_map/all_to_all | solution.py:42
  46.5 14.1 %all-to-all-start.2 = ((bf16[64,2,8]{2,1,0:T(2,128)(2,1)}), bf16[64,2,8]{2,1,0:T(2,128)(2,1)S(1)}, u32[]{:S(2)}, u32[]{:S(2)}) async-start(bf16[64,2,8]{2,1,0:T(2,128)(2,1)} %bitcast.6), calls=%async_computation.2 | async-start | bytes 65536 | tf_op jit(solution)/shard_map/all_to_all | solution.py:41
  52.9 42.8 %all-gather.11.cloned.1.call-start = ((), (), s32[]{:S(2)}) async-start(), calls=%async_computation.4 | async-start | bytes 2621440 | tf_op jit(solution)/shard_map/all_gather | solution.py:63
  65.4 69.9 %all-gather.13.cloned.1.call-start = ((), (), s32[]{:S(2)}) async-start(), calls=%async_computation.5 | async-start | bytes 2621440 | tf_op jit(solution)/shard_map/all_gather | solution.py:69
  101.7 108.9 %all-gather.15.cloned.1.call-start = ((), (), s32[]{:S(2)}) async-start(), calls=%async_computation.6 | async-start | bytes 2621440 | tf_op jit(solution)/shard_map/all_gather | solution.py:80
  135.3 29.7 %collective-permute-start = (bf16[4,512,512]{2,1,0:T(8,128)(2,1)}, bf16[4,512,512]{2,1,0:T(8,128)(2,1)S(1)}, u32[]{:S(2)}, u32[]{:S(2)}) collective-permute-start(bf16[4,512,512]{2,1,0:T(8,128)(2,1)} %all-gather.13.cloned.1.call-done), channel_id=1, source_target_pairs={{0,4},{4,8},{8,12},{12,16},{16,20},{20,24},{24,28},{28,32},{32,36}... | collective-permute-start | bytes 6291464 | tf_op jit(solution)/shard_map/ppermute | solution.py:13
  178.0 86.0 %copy-start.1 = (bf16[4,128,512]{2,1,0:T(8,128)(2,1)S(1)}, bf16[4,128,512]{2,1,0:T(8,128)(2,1)}, u32[]{:S(2)}) copy-start(bf16[4,128,512]{2,1,0:T(8,128)(2,1)} %maximum_select_fusion) | copy-start | bytes 1572868
  178.0 130.1 %all-gather.17.cloned.1.call-start = ((), (), s32[]{:S(2)}) async-start(), calls=%async_computation.7 | async-start | bytes 2621440 | tf_op jit(solution)/shard_map/all_gather | solution.py:80
  210.7 51.7 %collective-permute-start.1 = (bf16[4,512,512]{2,1,0:T(8,128)(2,1)}, bf16[4,512,512]{2,1,0:T(8,128)(2,1)}, u32[]{:S(2)}, u32[]{:S(2)}) collective-permute-start(bf16[4,512,512]{2,1,0:T(8,128)(2,1)} %all-gather.15.cloned.1.call-done), channel_id=1, source_target_pairs={{0,8},{4,12},{8,16},{12,20},{16,24},{20,28},{24,32},{28,36},{32,40... | collective-permute-start | bytes 6291464 | tf_op jit(solution)/shard_map/ppermute | solution.py:13
  275.4 132.7 %copy-start.2 = (bf16[4,128,512]{2,1,0:T(8,128)(2,1)S(1)}, bf16[4,128,512]{2,1,0:T(8,128)(2,1)}, u32[]{:S(2)}) copy-start(bf16[4,128,512]{2,1,0:T(8,128)(2,1)} %maximum_select_fusion.1) | copy-start | bytes 1572868
  275.4 178.2 %all-gather.19.cloned.1.call-start = ((), (), s32[]{:S(2)}) async-start(), calls=%async_computation.8 | async-start | bytes 2621440 | tf_op jit(solution)/shard_map/all_gather | solution.py:80
  308.1 98.4 %collective-permute-start.2 = (bf16[4,512,512]{2,1,0:T(8,128)(2,1)}, bf16[4,512,512]{2,1,0:T(8,128)(2,1)}, u32[]{:S(2)}, u32[]{:S(2)}) collective-permute-start(bf16[4,512,512]{2,1,0:T(8,128)(2,1)} %all-gather.17.cloned.1.call-done), channel_id=1, source_target_pairs={{0,16},{4,20},{8,24},{12,28},{16,32},{20,36},{24,40},{28,44},{32,4... | collective-permute-start | bytes 6291464 | tf_op jit(solution)/shard_map/ppermute | solution.py:13
  420.9 122.8 %copy-start.3 = (bf16[4,128,512]{2,1,0:T(8,128)(2,1)S(1)}, bf16[4,128,512]{2,1,0:T(8,128)(2,1)}, u32[]{:S(2)}) copy-start(bf16[4,128,512]{2,1,0:T(8,128)(2,1)} %maximum_select_fusion.2) | copy-start | bytes 1572868
  420.9 182.4 %all-gather.21.cloned.1.call-start = ((), (), s32[]{:S(2)}) async-start(), calls=%async_computation.9 | async-start | bytes 2621440 | tf_op jit(solution)/shard_map/all_gather | solution.py:80
  453.6 88.5 %collective-permute-start.3 = (bf16[4,512,512]{2,1,0:T(8,128)(2,1)}, bf16[4,512,512]{2,1,0:T(8,128)(2,1)}, u32[]{:S(2)}, u32[]{:S(2)}) collective-permute-start(bf16[4,512,512]{2,1,0:T(8,128)(2,1)} %all-gather.19.cloned.1.call-done), channel_id=1, source_target_pairs={{0,32},{4,36},{8,40},{12,44},{16,48},{20,52},{24,56},{28,60},{32,6... | collective-permute-start | bytes 6291464 | tf_op jit(solution)/shard_map/ppermute | solution.py:13
  559.1 95.4 %copy-start.4 = (bf16[4,128,512]{2,1,0:T(8,128)(2,1)S(1)}, bf16[4,128,512]{2,1,0:T(8,128)(2,1)}, u32[]{:S(2)}) copy-start(bf16[4,128,512]{2,1,0:T(8,128)(2,1)} %maximum_select_fusion.3) | copy-start | bytes 1572868
  559.2 147.3 %all-gather.23.cloned.1.call-start = ((), (), s32[]{:S(2)}) async-start(), calls=%async_computation.10 | async-start | bytes 2621440 | tf_op jit(solution)/shard_map/all_gather | solution.py:80
  603.4 49.6 %collective-permute-start.4 = (bf16[4,512,512]{2,1,0:T(8,128)(2,1)}, bf16[4,512,512]{2,1,0:T(8,128)(2,1)}, u32[]{:S(2)}, u32[]{:S(2)}) collective-permute-start(bf16[4,512,512]{2,1,0:T(8,128)(2,1)} %all-gather.21.cloned.1.call-done), channel_id=1, source_target_pairs={{0,64},{4,68},{8,72},{12,76},{16,80},{20,84},{24,88},{28,92},{32,9... | collective-permute-start | bytes 6291464 | tf_op jit(solution)/shard_map/ppermute | solution.py:13
  662.0 8.7 %copy-start.10 = (bf16[128,512]{1,0:T(8,128)(2,1)S(1)}, bf16[128,512]{1,0:T(8,128)(2,1)}, u32[]{:S(2)}) copy-start(bf16[128,512]{1,0:T(8,128)(2,1)} %copy-done.9) | copy-start | bytes 393220
  662.0 8.7 %copy-start.13 = (bf16[128,512]{1,0:T(8,128)(2,1)S(1)}, bf16[128,512]{1,0:T(8,128)(2,1)}, u32[]{:S(2)}) copy-start(bf16[128,512]{1,0:T(8,128)(2,1)} %copy-done.12) | copy-start | bytes 393220
  662.0 8.7 %copy-start.16 = (bf16[128,512]{1,0:T(8,128)(2,1)S(1)}, bf16[128,512]{1,0:T(8,128)(2,1)}, u32[]{:S(2)}) copy-start(bf16[128,512]{1,0:T(8,128)(2,1)} %copy-done.15) | copy-start | bytes 393220
  672.8 86.3 %copy-start = (bf16[4,128,512]{2,1,0:T(8,128)(2,1)S(1)}, bf16[4,128,512]{2,1,0:T(8,128)(2,1)}, u32[]{:S(2)}) copy-start(bf16[4,128,512]{2,1,0:T(8,128)(2,1)} %maximum_select_fusion.4) | copy-start | bytes 1572868
  706.4 51.1 %collective-permute-start.5 = (bf16[4,512,512]{2,1,0:T(8,128)(2,1)}, bf16[4,512,512]{2,1,0:T(8,128)(2,1)}, u32[]{:S(2)}, u32[]{:S(2)}) collective-permute-start(bf16[4,512,512]{2,1,0:T(8,128)(2,1)} %all-gather.23.cloned.1.call-done), channel_id=1, source_target_pairs={{0,128},{4,132},{8,136},{12,140},{16,144},{20,148},{24,152},{28,15... | collective-permute-start | bytes 6291464 | tf_op jit(solution)/shard_map/ppermute | solution.py:13
  (15 other events, 72.3 us)
Sparse Core Ops, SparseCore 0:
  31.0 25.5 all-gather.8
  65.5 30.0 all-gather.10
  101.9 33.4 all-gather.12
  178.1 32.5 all-gather.14
  275.5 32.5 all-gather.16
  421.0 32.5 all-gather.18
  559.3 44.0 all-gather.20
  673.0 33.4 all-gather.22
where the time goes:
time: 786 us; the launch traced here: 784 us
  waiting for transfers between devices  600 us (76%)
  matrix products  86.9 us (11%)
  starting transfers between devices  35.1 us (4%)
  blocking collectives  23.6 us (3%)
  between operations  14.3 us (2%)
  local copies, waits for them, and re-layouts  13.7 us (2%)
  other arithmetic  10.2 us (1%)
    ppermute x6, waiting for transfers between devices, passed_along(): lax.ppermute(value, axis, [(source, source + steps) for source in range(f...  347 us
    all_gather x6, waiting for transfers between devices, on_device(): full_now = lax.all_gather(rows_now, 'blk', axis=1, tiled=True)  209 us
    dot_general x70, matrix products, times_f32(): return jnp.dot(left_op, right_op, preferred_element_type=jnp.float32)  83.3 us
    all_gather x1, waiting for transfers between devices, on_device(): lax.all_gather(jnp.stack([refl_rows, tran_rows], axis=1), 'blk', axis=2,...  30.2 us
    all_to_all x1, blocking collectives, on_device(): lax.all_to_all(mode_matrix, 'layer', split_axis=0, concat_axis=1, tiled=T...  23.6 us
    ppermute x6, starting transfers between devices, passed_along(): lax.ppermute(value, axis, [(source, source + steps) for source in range(f...  22 us
  transfers between devices with their start and end apart: 16, of which 15 were waited for; matrix products, arithmetic and copies ran while one was open for 0% of the time, Pallas kernels for 0%

commit v1 on v0

--- a/solution.py
+++ b/solution.py
@@ -5,6 +5,27 @@
 
 HARM = 512
 REFL = 4
+
+
+def ring_gather(x, axis, dim):
+    peers, index, rows = (lax.axis_size(axis), lax.axis_index(axis), x.shape[dim])
+    right = [(i, (i + 1) % peers) for i in range(peers)]
+    left = [(i, (i - 1) % peers) for i in range(peers)]
+    result = jnp.zeros((*x.shape[:dim], peers * rows, *x.shape[dim + 1 :]), x.dtype)
+    result = lax.dynamic_update_slice_in_dim(result, x, index * rows, axis=dim)
+    from_left = from_right = x
+    middle = peers // 2
+    for step in range(1, middle + 1):
+        from_left = lax.ppermute(from_left, axis, right)
+        result = lax.dynamic_update_slice_in_dim(
+            result, from_left, (index - step) % peers * rows, axis=dim
+        )
+        if step < peers - middle:
+            from_right = lax.ppermute(from_right, axis, left)
+            result = lax.dynamic_update_slice_in_dim(
+                result, from_right, (index + step) % peers * rows, axis=dim
+            )
+    return result
 
 
 def passed_along(value, axis, steps):
@@ -77,7 +98,7 @@
         combined = star_rows(upper_near, upper_far, full_now[0:2], rows_now[2:4])
         rows_now = jnp.where(group_index >= distance, combined, rows_now)
         if section_level + 1 < level_count:
-            full_now = lax.all_gather(rows_now, "blk", axis=1, tiled=True)
+            full_now = ring_gather(rows_now, "blk", 1)
     return rows_now[None]
 
 

time: 786 us -> 725 us (0.922); the launches traced: 784 us -> 714 us
  waiting for transfers between devices: 600 us -> 497 us
  starting transfers between devices: 35.1 us -> 61.9 us
  local copies, waits for them, and re-layouts: 13.7 us -> 29.9 us
    all_gather x6 -> x1, waiting for transfers between devices: 209 us -> 33.6 us  [on_device(): full_now = lax.all_gather(rows_now, 'blk', axis=1, tiled=True)]
    ppermute x0 -> x15, waiting for transfers between devices: none -> 99.5 us  [the longest x10 99.5 us: ring_gather(): from_left = lax.ppermute(from_left, axis, right)]
    ppermute x6, waiting for transfers between devices: 347 us -> 320 us  [passed_along(): lax.ppermute(value, axis, [(source, source + steps) for source in range(f...]
    ppermute x0 -> x15, starting transfers between devices: none -> 16.4 us  [the longest x5 15.6 us: ring_gather(): from_right = lax.ppermute(from_right, axis, left)]
    dynamic_update_slice x0 -> x15, local copies, waits for them, and re-layouts: none -> 10.9 us  [the longest x10 7.29 us: ring_gather(): lax.dynamic_update_slice_in_dim(result, from_left, (index - step) % peers...]
    ppermute x6, starting transfers between devices: 22 us -> 32.6 us  [passed_along(): lax.ppermute(value, axis, [(source, source + steps) for source in range(f...]
  transfers between devices with their start and end apart: 16 -> 26, of which waited for: 15 -> 20; matrix products, arithmetic and copies ran while one was open for 0% -> 1% of each run, Pallas kernels for 0% -> 0%
where the time goes in v1:
time: 725 us; the launch traced here: 714 us
  waiting for transfers between devices  497 us (69%)
  matrix products  79.1 us (11%)
  starting transfers between devices  61.9 us (9%)
  local copies, waits for them, and re-layouts  29.9 us (4%)
  blocking collectives  23.6 us (3%)
  between operations  14.2 us (2%)
  other arithmetic  7.64 us (1%)
    ppermute x6, waiting for transfers between devices, passed_along(): lax.ppermute(value, axis, [(source, source + steps) for source in range(f...  320 us
    ppermute x10, waiting for transfers between devices, ring_gather(): from_left = lax.ppermute(from_left, axis, right)  99.5 us
    dot_general x70, matrix products, times_f32(): return jnp.dot(left_op, right_op, preferred_element_type=jnp.float32)  75.4 us
    all_gather x1, waiting for transfers between devices, on_device(): full_now = lax.all_gather(rows_now, 'blk', axis=1, tiled=True)  33.6 us
    ppermute x6, starting transfers between devices, passed_along(): lax.ppermute(value, axis, [(source, source + steps) for source in range(f...  32.6 us
    all_gather x1, waiting for transfers between devices, on_device(): lax.all_gather(jnp.stack([refl_rows, tran_rows], axis=1), 'blk', axis=2,...  30.2 us
    all_to_all x1, blocking collectives, on_device(): lax.all_to_all(mode_matrix, 'layer', split_axis=0, concat_axis=1, tiled=T...  23.6 us
    ppermute x5, starting transfers between devices, ring_gather(): from_right = lax.ppermute(from_right, axis, left)  15.6 us
  transfers between devices with their start and end apart: 26, of which 20 were waited for; matrix products, arithmetic and copies ran while one was open for 1% of the time, Pallas kernels for 0%

profile of v1, /device:TPU:16, one launch (start us, length us, event | category | flops | bytes accessed | tf_op | source)
XLA Modules:
  0.0 713.5 jit_solution(448048660947568460)
XLA Ops:
  6.5 23.6 %all_to_all.44 = bf16[128,8,128]{2,1,0:T(8,128)(2,1)S(1)} all-to-all(bf16[128,8,128]{2,1,0:T(8,128)(2,1)} %param.3), channel_id=1, replica_groups=mesh['layer'=64,'blk'=4] {'layer'}, dimensions={0} | all-to-all | bytes 524288 | tf_op jit(solution)/shard_map/all_to_all | solution.py:61
  32.3 6.5 all-to-all-start.1
  46.5 6.4 all-to-all-start.2
  53.0 7.5 %all-to-all-done.2 = bf16[64,2,8]{2,1,0:T(2,128)(2,1)S(1)} async-done(((bf16[64,2,8]{2,1,0:T(2,128)(2,1)}), bf16[64,2,8]{2,1,0:T(2,128)(2,1)S(1)}, u32[]{:S(2)}, u32[]{:S(2)}) %all-to-all-start.2) | async-done | bytes 2080 | tf_op jit(solution)/shard_map/all_to_all | solution.py:62
  65.4 30.2 %all-gather.6.cloned.1.call-done = bf16[2,2,512,512]{3,2,0,1:T(8,128)(2,1)} async-done(((bf16[2,2,128,512]{3,2,0,1:T(8,128)(2,1)}), bf16[2,2,512,512]{3,2,0,1:T(8,128)(2,1)}) %all-gather.6.cloned.1.call-update) | async-done | bytes 2097168 | tf_op jit(solution)/shard_map/all_gather | solution.py:84
  101.8 33.6 %all-gather.8.cloned.1.call-done = bf16[4,512,512]{2,1,0:T(8,128)(2,1)} async-done(((bf16[4,128,512]{2,1,0:T(8,128)(2,1)}), bf16[4,512,512]{2,1,0:T(8,128)(2,1)}) %all-gather.8.cloned.1.call-update) | async-done | bytes 2097168 | tf_op jit(solution)/shard_map/all_gather | solution.py:90
  137.3 27.8 %collective-permute-done = bf16[4,512,512]{2,1,0:T(8,128)(2,1)} collective-permute-done((bf16[4,512,512]{2,1,0:T(8,128)(2,1)}, bf16[4,512,512]{2,1,0:T(8,128)(2,1)}, u32[]{:S(2)}, u32[]{:S(2)}) %collective-permute-start) | collective-permute-done | bytes 2097184 | tf_op jit(solution)/shard_map/ppermute | solution.py:34
  182.3 9.0 %collective-permute-done.1 = bf16[4,128,512]{2,1,0:T(8,128)(2,1)} collective-permute-done((bf16[4,128,512]{2,1,0:T(8,128)(2,1)S(1)}, bf16[4,128,512]{2,1,0:T(8,128)(2,1)}, u32[]{:S(2)}, u32[]{:S(2)}) %collective-permute-start.1) | collective-permute-done | bytes 524320 | tf_op jit(solution)/shard_map/ppermute | solution.py:19
  193.5 9.3 %collective-permute-done.3 = bf16[4,128,512]{2,1,0:T(8,128)(2,1)} collective-permute-done((bf16[4,128,512]{2,1,0:T(8,128)(2,1)}, bf16[4,128,512]{2,1,0:T(8,128)(2,1)}, u32[]{:S(2)}, u32[]{:S(2)}) %collective-permute-start.3) | collective-permute-done | bytes 524320 | tf_op jit(solution)/shard_map/ppermute | solution.py:19
  209.7 42.7 %collective-permute-done.4 = bf16[4,512,512]{2,1,0:T(8,128)(2,1)} collective-permute-done((bf16[4,512,512]{2,1,0:T(8,128)(2,1)S(1)}, bf16[4,512,512]{2,1,0:T(8,128)(2,1)}, u32[]{:S(2)}, u32[]{:S(2)}) %collective-permute-start.4) | collective-permute-done | bytes 2097184 | tf_op jit(solution)/shard_map/ppermute | solution.py:34
  270.4 8.9 %collective-permute-done.5 = bf16[4,128,512]{2,1,0:T(8,128)(2,1)S(1)} collective-permute-done((bf16[4,128,512]{2,1,0:T(8,128)(2,1)S(1)}, bf16[4,128,512]{2,1,0:T(8,128)(2,1)S(1)}, u32[]{:S(2)}, u32[]{:S(2)}) %collective-permute-start.5) | collective-permute-done | bytes 524320 | tf_op jit(solution)/shard_map/ppermute | solution.py:19
  280.9 8.7 %collective-permute-done.7 = bf16[4,128,512]{2,1,0:T(8,128)(2,1)S(1)} collective-permute-done((bf16[4,128,512]{2,1,0:T(8,128)(2,1)S(1)}, bf16[4,128,512]{2,1,0:T(8,128)(2,1)S(1)}, u32[]{:S(2)}, u32[]{:S(2)}) %collective-permute-start.7) | collective-permute-done | bytes 524320 | tf_op jit(solution)/shard_map/ppermute | solution.py:19
  290.4 10.3 %collective-permute-start.8 = (bf16[4,512,512]{2,1,0:T(8,128)(2,1)}, bf16[4,512,512]{2,1,0:T(8,128)(2,1)}, u32[]{:S(2)}, u32[]{:S(2)}) collective-permute-start(bf16[4,512,512]{2,1,0:T(8,128)(2,1)} %constant_dynamic-update-slice_fusion.12), channel_id=1, source_target_pairs={{0,16},{4,20},{8,24},{12,28},{16,32},{20,36},{24,40},{28,44},{32,4... | collective-permute-start | bytes 6291464 | tf_op jit(solution)/shard_map/ppermute | solution.py:34
  300.7 80.3 %collective-permute-done.8 = bf16[4,512,512]{2,1,0:T(8,128)(2,1)} collective-permute-done((bf16[4,512,512]{2,1,0:T(8,128)(2,1)}, bf16[4,512,512]{2,1,0:T(8,128)(2,1)}, u32[]{:S(2)}, u32[]{:S(2)}) %collective-permute-start.8) | collective-permute-done | bytes 2097184 | tf_op jit(solution)/shard_map/ppermute | solution.py:34
  398.9 11.8 %collective-permute-done.9 = bf16[4,128,512]{2,1,0:T(8,128)(2,1)S(1)} collective-permute-done((bf16[4,128,512]{2,1,0:T(8,128)(2,1)S(1)}, bf16[4,128,512]{2,1,0:T(8,128)(2,1)S(1)}, u32[]{:S(2)}, u32[]{:S(2)}) %collective-permute-start.9) | collective-permute-done | bytes 524320 | tf_op jit(solution)/shard_map/ppermute | solution.py:19
  412.4 12.5 %collective-permute-done.11 = bf16[4,128,512]{2,1,0:T(8,128)(2,1)S(1)} collective-permute-done((bf16[4,128,512]{2,1,0:T(8,128)(2,1)S(1)}, bf16[4,128,512]{2,1,0:T(8,128)(2,1)S(1)}, u32[]{:S(2)}, u32[]{:S(2)}) %collective-permute-start.11) | collective-permute-done | bytes 524320 | tf_op jit(solution)/shard_map/ppermute | solution.py:19
  425.7 11.4 %collective-permute-start.12 = (bf16[4,512,512]{2,1,0:T(8,128)(2,1)}, bf16[4,512,512]{2,1,0:T(8,128)(2,1)}, u32[]{:S(2)}, u32[]{:S(2)}) collective-permute-start(bf16[4,512,512]{2,1,0:T(8,128)(2,1)} %constant_dynamic-update-slice_fusion.8), channel_id=1, source_target_pairs={{0,32},{4,36},{8,40},{12,44},{16,48},{20,52},{24,56},{28,60},{32,6... | collective-permute-start | bytes 6291464 | tf_op jit(solution)/shard_map/ppermute | solution.py:34
  437.1 87.1 %collective-permute-done.12 = bf16[4,512,512]{2,1,0:T(8,128)(2,1)} collective-permute-done((bf16[4,512,512]{2,1,0:T(8,128)(2,1)}, bf16[4,512,512]{2,1,0:T(8,128)(2,1)}, u32[]{:S(2)}, u32[]{:S(2)}) %collective-permute-start.12) | collective-permute-done | bytes 2097184 | tf_op jit(solution)/shard_map/ppermute | solution.py:34
  542.2 8.9 %collective-permute-done.13 = bf16[4,128,512]{2,1,0:T(8,128)(2,1)S(1)} collective-permute-done((bf16[4,128,512]{2,1,0:T(8,128)(2,1)S(1)}, bf16[4,128,512]{2,1,0:T(8,128)(2,1)S(1)}, u32[]{:S(2)}, u32[]{:S(2)}) %collective-permute-start.13) | collective-permute-done | bytes 524320 | tf_op jit(solution)/shard_map/ppermute | solution.py:19
  552.7 8.7 %collective-permute-done.15 = bf16[4,128,512]{2,1,0:T(8,128)(2,1)S(1)} collective-permute-done((bf16[4,128,512]{2,1,0:T(8,128)(2,1)S(1)}, bf16[4,128,512]{2,1,0:T(8,128)(2,1)S(1)}, u32[]{:S(2)}, u32[]{:S(2)}) %collective-permute-start.15) | collective-permute-done | bytes 524320 | tf_op jit(solution)/shard_map/ppermute | solution.py:19
  564.2 41.6 %collective-permute-done.16 = bf16[4,512,512]{2,1,0:T(8,128)(2,1)} collective-permute-done((bf16[4,512,512]{2,1,0:T(8,128)(2,1)}, bf16[4,512,512]{2,1,0:T(8,128)(2,1)}, u32[]{:S(2)}, u32[]{:S(2)}) %collective-permute-start.16) | collective-permute-done | bytes 2097184 | tf_op jit(solution)/shard_map/ppermute | solution.py:34
  623.1 11.5 %collective-permute-done.17 = bf16[4,128,512]{2,1,0:T(8,128)(2,1)S(1)} collective-permute-done((bf16[4,128,512]{2,1,0:T(8,128)(2,1)S(1)}, bf16[4,128,512]{2,1,0:T(8,128)(2,1)S(1)}, u32[]{:S(2)}, u32[]{:S(2)}) %collective-permute-start.17) | collective-permute-done | bytes 524320 | tf_op jit(solution)/shard_map/ppermute | solution.py:19
  634.7 10.3 %collective-permute-done.19 = bf16[4,128,512]{2,1,0:T(8,128)(2,1)S(1)} collective-permute-done((bf16[4,128,512]{2,1,0:T(8,128)(2,1)S(1)}, bf16[4,128,512]{2,1,0:T(8,128)(2,1)S(1)}, u32[]{:S(2)}, u32[]{:S(2)}) %collective-permute-start.19) | collective-permute-done | bytes 524320 | tf_op jit(solution)/shard_map/ppermute | solution.py:19
  646.4 40.4 %collective-permute-done.20 = bf16[4,512,512]{2,1,0:T(8,128)(2,1)} collective-permute-done((bf16[4,512,512]{2,1,0:T(8,128)(2,1)S(1)}, bf16[4,512,512]{2,1,0:T(8,128)(2,1)}, u32[]{:S(2)}, u32[]{:S(2)}) %collective-permute-start.20) | collective-permute-done | bytes 2097184 | tf_op jit(solution)/shard_map/ppermute | solution.py:34
  (203 shorter events, 150.4 us)
Async XLA Ops:
  6.5 54.4 %all-gather.4.cloned.1.call-start = ((), (), s32[]{:S(2)}) async-start(), calls=%async_computation.3 | async-start | bytes 1310720 | tf_op jit(solution)/shard_map/all_gather | solution.py:70
  32.3 14.2 %all-to-all-start.1 = ((bf16[64,2,8]{2,1,0:T(2,128)(2,1)}), bf16[64,2,8]{2,1,0:T(2,128)(2,1)S(1)}, u32[]{:S(2)}, u32[]{:S(2)}) async-start(bf16[64,2,8]{2,1,0:T(2,128)(2,1)} %bitcast.3), calls=%async_computation.1 | async-start | bytes 65536 | tf_op jit(solution)/shard_map/all_to_all | solution.py:63
  46.5 14.1 %all-to-all-start.2 = ((bf16[64,2,8]{2,1,0:T(2,128)(2,1)}), bf16[64,2,8]{2,1,0:T(2,128)(2,1)S(1)}, u32[]{:S(2)}, u32[]{:S(2)}) async-start(bf16[64,2,8]{2,1,0:T(2,128)(2,1)} %bitcast.6), calls=%async_computation.2 | async-start | bytes 65536 | tf_op jit(solution)/shard_map/all_to_all | solution.py:62
  52.8 42.8 %all-gather.6.cloned.1.call-start = ((), (), s32[]{:S(2)}) async-start(), calls=%async_computation.4 | async-start | bytes 2621440 | tf_op jit(solution)/shard_map/all_gather | solution.py:84
  65.4 70.0 %all-gather.8.cloned.1.call-start = ((), (), s32[]{:S(2)}) async-start(), calls=%async_computation.5 | async-start | bytes 2621440 | tf_op jit(solution)/shard_map/all_gather | solution.py:90
  135.3 29.8 %collective-permute-start = (bf16[4,512,512]{2,1,0:T(8,128)(2,1)}, bf16[4,512,512]{2,1,0:T(8,128)(2,1)}, u32[]{:S(2)}, u32[]{:S(2)}) collective-permute-start(bf16[4,512,512]{2,1,0:T(8,128)(2,1)} %all-gather.8.cloned.1.call-done), channel_id=1, source_target_pairs={{0,4},{4,8},{8,12},{12,16},{16,20},{20,24},{24,28},{28,32},{32,36}... | collective-permute-start | bytes 6291464 | tf_op jit(solution)/shard_map/ppermute | solution.py:34
  179.0 12.3 %collective-permute-start.1 = (bf16[4,128,512]{2,1,0:T(8,128)(2,1)S(1)}, bf16[4,128,512]{2,1,0:T(8,128)(2,1)}, u32[]{:S(2)}, u32[]{:S(2)}) collective-permute-start(bf16[4,128,512]{2,1,0:T(8,128)(2,1)S(1)} %get-tuple-element.14), channel_id=1, source_target_pairs={{0,1},{1,2},{2,3},{3,0},{4,5},{5,6},{6,7},{7,4},{8,9},{9,10},{10,1... | collective-permute-start | bytes 1572872 | tf_op jit(solution)/shard_map/ppermute | solution.py:19
  179.6 12.8 %collective-permute-start.2 = (bf16[4,128,512]{2,1,0:T(8,128)(2,1)S(1)}, bf16[4,128,512]{2,1,0:T(8,128)(2,1)}, u32[]{:S(2)}, u32[]{:S(2)}) collective-permute-start(bf16[4,128,512]{2,1,0:T(8,128)(2,1)S(1)} %get-tuple-element.14), channel_id=1, source_target_pairs={{0,3},{1,0},{2,1},{3,2},{4,7},{5,4},{6,5},{7,6},{8,11},{9,8},{10,9... | collective-permute-start | bytes 1572872 | tf_op jit(solution)/shard_map/ppermute | solution.py:24
  191.3 11.5 %collective-permute-start.3 = (bf16[4,128,512]{2,1,0:T(8,128)(2,1)}, bf16[4,128,512]{2,1,0:T(8,128)(2,1)}, u32[]{:S(2)}, u32[]{:S(2)}) collective-permute-start(bf16[4,128,512]{2,1,0:T(8,128)(2,1)} %collective-permute-done.1), channel_id=1, source_target_pairs={{0,1},{1,2},{2,3},{3,0},{4,5},{5,6},{6,7},{7,4},{8,9},{9,10},{10,1... | collective-permute-start | bytes 1572872 | tf_op jit(solution)/shard_map/ppermute | solution.py:19
  203.9 48.4 %collective-permute-start.4 = (bf16[4,512,512]{2,1,0:T(8,128)(2,1)S(1)}, bf16[4,512,512]{2,1,0:T(8,128)(2,1)}, u32[]{:S(2)}, u32[]{:S(2)}) collective-permute-start(bf16[4,512,512]{2,1,0:T(8,128)(2,1)S(1)} %constant_dynamic-update-slice_fusion.16), channel_id=1, source_target_pairs={{0,8},{4,12},{8,16},{12,20},{16,24},{20,28},{24,32},{28,36},{32,40... | collective-permute-start | bytes 6291464 | tf_op jit(solution)/shard_map/ppermute | solution.py:34
  267.1 12.2 %collective-permute-start.5 = (bf16[4,128,512]{2,1,0:T(8,128)(2,1)S(1)}, bf16[4,128,512]{2,1,0:T(8,128)(2,1)S(1)}, u32[]{:S(2)}, u32[]{:S(2)}) collective-permute-start(bf16[4,128,512]{2,1,0:T(8,128)(2,1)S(1)} %get-tuple-element.12), channel_id=1, source_target_pairs={{0,1},{1,2},{2,3},{3,0},{4,5},{5,6},{6,7},{7,4},{8,9},{9,10},{10,1... | collective-permute-start | bytes 1572872 | tf_op jit(solution)/shard_map/ppermute | solution.py:19
  267.1 12.9 %collective-permute-start.6 = (bf16[4,128,512]{2,1,0:T(8,128)(2,1)S(1)}, bf16[4,128,512]{2,1,0:T(8,128)(2,1)S(1)}, u32[]{:S(2)}, u32[]{:S(2)}) collective-permute-start(bf16[4,128,512]{2,1,0:T(8,128)(2,1)S(1)} %get-tuple-element.12), channel_id=1, source_target_pairs={{0,3},{1,0},{2,1},{3,2},{4,7},{5,4},{6,5},{7,6},{8,11},{9,8},{10,9... | collective-permute-start | bytes 1572872 | tf_op jit(solution)/shard_map/ppermute | solution.py:24
  279.2 10.4 %collective-permute-start.7 = (bf16[4,128,512]{2,1,0:T(8,128)(2,1)S(1)}, bf16[4,128,512]{2,1,0:T(8,128)(2,1)S(1)}, u32[]{:S(2)}, u32[]{:S(2)}) collective-permute-start(bf16[4,128,512]{2,1,0:T(8,128)(2,1)S(1)} %collective-permute-done.5), channel_id=1, source_target_pairs={{0,1},{1,2},{2,3},{3,0},{4,5},{5,6},{6,7},{7,4},{8,9},{9,10},{10,1... | collective-permute-start | bytes 1572872 | tf_op jit(solution)/shard_map/ppermute | solution.py:19
  290.4 90.6 %collective-permute-start.8 = (bf16[4,512,512]{2,1,0:T(8,128)(2,1)}, bf16[4,512,512]{2,1,0:T(8,128)(2,1)}, u32[]{:S(2)}, u32[]{:S(2)}) collective-permute-start(bf16[4,512,512]{2,1,0:T(8,128)(2,1)} %constant_dynamic-update-slice_fusion.12), channel_id=1, source_target_pairs={{0,16},{4,20},{8,24},{12,28},{16,32},{20,36},{24,40},{28,44},{32,4... | collective-permute-start | bytes 6291464 | tf_op jit(solution)/shard_map/ppermute | solution.py:34
  395.7 15.0 %collective-permute-start.9 = (bf16[4,128,512]{2,1,0:T(8,128)(2,1)S(1)}, bf16[4,128,512]{2,1,0:T(8,128)(2,1)S(1)}, u32[]{:S(2)}, u32[]{:S(2)}) collective-permute-start(bf16[4,128,512]{2,1,0:T(8,128)(2,1)S(1)} %get-tuple-element.10), channel_id=1, source_target_pairs={{0,1},{1,2},{2,3},{3,0},{4,5},{5,6},{6,7},{7,4},{8,9},{9,10},{10,1... | collective-permute-start | bytes 1572872 | tf_op jit(solution)/shard_map/ppermute | solution.py:19
  395.7 15.8 %collective-permute-start.10 = (bf16[4,128,512]{2,1,0:T(8,128)(2,1)S(1)}, bf16[4,128,512]{2,1,0:T(8,128)(2,1)S(1)}, u32[]{:S(2)}, u32[]{:S(2)}) collective-permute-start(bf16[4,128,512]{2,1,0:T(8,128)(2,1)S(1)} %get-tuple-element.10), channel_id=1, source_target_pairs={{0,3},{1,0},{2,1},{3,2},{4,7},{5,4},{6,5},{7,6},{8,11},{9,8},{10,9... | collective-permute-start | bytes 1572872 | tf_op jit(solution)/shard_map/ppermute | solution.py:24
  410.7 14.1 %collective-permute-start.11 = (bf16[4,128,512]{2,1,0:T(8,128)(2,1)S(1)}, bf16[4,128,512]{2,1,0:T(8,128)(2,1)S(1)}, u32[]{:S(2)}, u32[]{:S(2)}) collective-permute-start(bf16[4,128,512]{2,1,0:T(8,128)(2,1)S(1)} %collective-permute-done.9), channel_id=1, source_target_pairs={{0,1},{1,2},{2,3},{3,0},{4,5},{5,6},{6,7},{7,4},{8,9},{9,10},{10,1... | collective-permute-start | bytes 1572872 | tf_op jit(solution)/shard_map/ppermute | solution.py:19
  425.7 98.6 %collective-permute-start.12 = (bf16[4,512,512]{2,1,0:T(8,128)(2,1)}, bf16[4,512,512]{2,1,0:T(8,128)(2,1)}, u32[]{:S(2)}, u32[]{:S(2)}) collective-permute-start(bf16[4,512,512]{2,1,0:T(8,128)(2,1)} %constant_dynamic-update-slice_fusion.8), channel_id=1, source_target_pairs={{0,32},{4,36},{8,40},{12,44},{16,48},{20,52},{24,56},{28,60},{32,6... | collective-permute-start | bytes 6291464 | tf_op jit(solution)/shard_map/ppermute | solution.py:34
  538.9 12.1 %collective-permute-start.13 = (bf16[4,128,512]{2,1,0:T(8,128)(2,1)S(1)}, bf16[4,128,512]{2,1,0:T(8,128)(2,1)S(1)}, u32[]{:S(2)}, u32[]{:S(2)}) collective-permute-start(bf16[4,128,512]{2,1,0:T(8,128)(2,1)S(1)} %get-tuple-element.8), channel_id=1, source_target_pairs={{0,1},{1,2},{2,3},{3,0},{4,5},{5,6},{6,7},{7,4},{8,9},{9,10},{10,1... | collective-permute-start | bytes 1572872 | tf_op jit(solution)/shard_map/ppermute | solution.py:19
  538.9 12.9 %collective-permute-start.14 = (bf16[4,128,512]{2,1,0:T(8,128)(2,1)S(1)}, bf16[4,128,512]{2,1,0:T(8,128)(2,1)S(1)}, u32[]{:S(2)}, u32[]{:S(2)}) collective-permute-start(bf16[4,128,512]{2,1,0:T(8,128)(2,1)S(1)} %get-tuple-element.8), channel_id=1, source_target_pairs={{0,3},{1,0},{2,1},{3,2},{4,7},{5,4},{6,5},{7,6},{8,11},{9,8},{10,9... | collective-permute-start | bytes 1572872 | tf_op jit(solution)/shard_map/ppermute | solution.py:24
  562.3 43.6 %collective-permute-start.16 = (bf16[4,512,512]{2,1,0:T(8,128)(2,1)}, bf16[4,512,512]{2,1,0:T(8,128)(2,1)}, u32[]{:S(2)}, u32[]{:S(2)}) collective-permute-start(bf16[4,512,512]{2,1,0:T(8,128)(2,1)} %constant_dynamic-update-slice_fusion.4), channel_id=1, source_target_pairs={{0,64},{4,68},{8,72},{12,76},{16,80},{20,84},{24,88},{28,92},{32,9... | collective-permute-start | bytes 6291464 | tf_op jit(solution)/shard_map/ppermute | solution.py:34
  619.8 14.8 %collective-permute-start.17 = (bf16[4,128,512]{2,1,0:T(8,128)(2,1)S(1)}, bf16[4,128,512]{2,1,0:T(8,128)(2,1)S(1)}, u32[]{:S(2)}, u32[]{:S(2)}) collective-permute-start(bf16[4,128,512]{2,1,0:T(8,128)(2,1)S(1)} %get-tuple-element.6), channel_id=1, source_target_pairs={{0,1},{1,2},{2,3},{3,0},{4,5},{5,6},{6,7},{7,4},{8,9},{9,10},{10,1... | collective-permute-start | bytes 1572872 | tf_op jit(solution)/shard_map/ppermute | solution.py:19
  619.9 14.8 %collective-permute-start.18 = (bf16[4,128,512]{2,1,0:T(8,128)(2,1)S(1)}, bf16[4,128,512]{2,1,0:T(8,128)(2,1)S(1)}, u32[]{:S(2)}, u32[]{:S(2)}) collective-permute-start(bf16[4,128,512]{2,1,0:T(8,128)(2,1)S(1)} %get-tuple-element.6), channel_id=1, source_target_pairs={{0,3},{1,0},{2,1},{3,2},{4,7},{5,4},{6,5},{7,6},{8,11},{9,8},{10,9... | collective-permute-start | bytes 1572872 | tf_op jit(solution)/shard_map/ppermute | solution.py:24
  645.1 41.7 %collective-permute-start.20 = (bf16[4,512,512]{2,1,0:T(8,128)(2,1)S(1)}, bf16[4,512,512]{2,1,0:T(8,128)(2,1)}, u32[]{:S(2)}, u32[]{:S(2)}) collective-permute-start(bf16[4,512,512]{2,1,0:T(8,128)(2,1)S(1)} %constant_dynamic-update-slice_fusion), channel_id=1, source_target_pairs={{0,128},{4,132},{8,136},{12,140},{16,144},{20,148},{24,152},{28,15... | collective-permute-start | bytes 6291464 | tf_op jit(solution)/shard_map/ppermute | solution.py:34
  (29 other events, 164.8 us)
Sparse Core Ops, SparseCore 0:
  31.0 25.5 all-gather.3
  65.5 30.1 all-gather.5
  101.9 33.4 all-gather.7
